TPU v7x, 128 devices: a whole 4x4x4 slice. The times are simulated.
128 devices in a mesh: mode: 8 (over x, core), member: 16 (over z, y).
Axes of the slice: x: 4, y: 4, z: 4, core: 2. Of those that a mesh axis runs over, the one named last changes fastest.
Arguments:
- ground_accel: bfloat16 [4, 639], replicated, may hold values from -6 to 6
- modal_kernel: bfloat16 [4096, 512], P(('mode', 'member')), may hold values from -0.25 to 0.25
- mode_shapes: bfloat16 [98304, 4096], P('member', 'mode'), may hold values from -0.09375 to 0.09375
- member_owner: int32 [16384, 1], P('member'), may hold values from 0 to 127; in each aligned block of 128 rows (0 to 127, 128 to 255, ...) at most 2 rows name the same one
- member_group: int32 [16384, 1], P('member'), may hold values from 0 to 3
- record_table: int32 [512, 8], P(('mode', 'member')), may hold values from 0 to 3
- case_coef: float32 [8, 6], replicated, may hold values from -1.5 to 1.5
- gravity: float32 [512, 8], P(('mode', 'member')), may hold values from -10 to 10
Outputs:
- demand: float32 [512, 8], P(('mode', 'member'))
Inputs may be any that keep to these rules, and one draw needn't show every extreme that they name: `member_owner`: in each aligned block of 1024 / 8 members no owner is named more than 2 times, a bound that some block reaches.
All inputs are finite; a program needn't handle non-finite values.
Results may differ from a plain program's by a relative error of at most 0.0065.
Values may be sent and summed in bfloat16 or wider, within the bound.
No kernel may reach another device: no remote copies, remote signals or barrier semaphores. Data moves between devices by JAX's collectives and lax.ppermute only.
A program may use at most 64 MiB of HBM per device.

v0:
```python
import jax
import jax.numpy as jnp
from jax import lax
from jax.sharding import PartitionSpec as P


def lagged_table(ground_accel, tap_count):
    record_count, span_len = ground_accel.shape
    step_count = span_len - tap_count + 1
    tiled = jnp.tile(ground_accel, (1, step_count + 1))[:, : step_count * (span_len + 1)]
    windows = tiled.reshape(record_count, step_count, span_len + 1)[:, :, :tap_count]
    return windows.reshape(record_count * step_count, tap_count)


def local(
    ground_accel,
    modal_kernel,
    mode_shapes,
    member_owner,
    member_group,
    record_table,
    case_coef,
    gravity,
):
    tap_count = modal_kernel.shape[1]
    record_count = ground_accel.shape[0]
    comp_count = case_coef.shape[1]
    n_mode = lax.axis_size("mode")
    n_member = lax.axis_size("member")
    groups_here = gravity.shape[0]
    group_total = groups_here * n_mode * n_member
    lagged = lagged_table(ground_accel, tap_count)
    local_resp = lax.dot_general(
        modal_kernel[:, ::-1], lagged, (((1,), (1,)), ((), ())), preferred_element_type=jnp.float32
    ).astype(jnp.bfloat16)
    modal_resp = lax.all_gather(local_resp, "member", axis=0, tiled=True)
    partial = jnp.dot(mode_shapes, modal_resp, preferred_element_type=jnp.float32).astype(
        jnp.bfloat16
    )
    members_here = member_owner.shape[0]
    packed = partial.reshape(members_here, comp_count * partial.shape[1])
    group_index = member_owner[:, 0] * groups_here + member_group[:, 0]
    selector = (jnp.arange(group_total)[:, None] == group_index[None, :]).astype(jnp.bfloat16)
    group_part = jnp.dot(selector, packed, preferred_element_type=jnp.float32)
    by_mode = lax.psum_scatter(
        group_part.astype(jnp.bfloat16), "mode", scatter_dimension=0, tiled=True
    )
    group_sums = lax.psum_scatter(
        by_mode.astype(jnp.float32), "member", scatter_dimension=0, tiled=True
    )
    group_sums = group_sums.reshape(groups_here, comp_count, record_count, -1)
    case_mix = jnp.einsum("sc,gcrt->gsrt", case_coef, group_sums, precision=lax.Precision.HIGHEST)
    record_pick = (record_table[:, :, None] == jnp.arange(record_count)[None, None, :]).astype(
        jnp.float32
    )
    selected = jnp.sum(record_pick[:, :, :, None] * case_mix, axis=2)
    combined = gravity[:, :, None] + selected
    return jnp.max(jnp.abs(combined), axis=2)


def solution(mesh):
    placed = (
        P(),
        P(("mode", "member"), None),
        P("member", "mode"),
        P("member", None),
        P("member", None),
        P(("mode", "member"), None),
        P(),
        P(("mode", "member"), None),
    )
    return jax.shard_map(
        local, mesh=mesh, in_specs=placed, out_specs=P(("mode", "member"), None), check_vma=False
    )
```

profile of v0, /device:TPU:0, one launch (start us, length us, event | category | flops | bytes accessed | tf_op | source)
XLA Modules:
  0.0 198.6 jit_solution(844657869856164750)
XLA Ops:
  6.5 0.0 copy-start
  6.5 0.0 reduce-scatter.2.cloned.1.call-start
  6.5 0.8 tile.4
  7.3 0.6 tile.10
  7.9 0.2 slice.8
  8.2 0.1 copy.21
  8.3 1.6 rev.3
  9.9 0.2 convolution_convert_fusion.2
  10.2 25.6 %all_gather.3 = bf16[512,512]{1,0:T(8,128)(2,1)S(1)} all-gather(bf16[32,512]{1,0:T(8,128)(2,1)S(1)} %convolution_convert_fusion.2), channel_id=1, replica_groups=mesh['mode'=8,'member'=16] {'member'}, dimensions={0}, use_global_device_ids=true | all-gather | bytes 557056 | tf_op jit(solution)/shard_map/all_gather | solution.py:36
  35.8 8.2 %fusion = bf16[6144,512]{0,1:T(8,128)(2,1)} fusion(bf16[512,512]{1,0:T(8,128)(2,1)S(1)} %all_gather.3, bf16[6144,512]{1,0:T(8,128)(2,1)} %param.10), kind=kOutput, calls=%fused_computation.1 | convolution fusion | flops 3224371200 | bytes 13107200 | tf_op jit(solution)/shard_map/dot_general | solution.py:37
  44.0 8.7 %copy.14 = bf16[6144,512]{1,0:T(8,128)(2,1)} copy(bf16[6144,512]{0,1:T(8,128)(2,1)} %fusion) | data formatting | bytes 12582912 | tf_op jit(solution)/shard_map/convert_element_type | solution.py:37
  52.7 0.0 copy-start.1
  52.7 0.0 copy-start.2
  52.7 11.5 %reshape.37 = bf16[1024,3072]{1,0:T(8,128)(2,1)} reshape(bf16[6144,512]{1,0:T(8,128)(2,1)} %copy.14) | data formatting | bytes 12582912 | tf_op jit(solution)/shard_map/reshape | solution.py:41
  64.2 0.0 copy-done.1
  64.2 0.0 copy-done.2
  64.2 0.0 copy-start.5
  64.2 0.0 copy-start.3
  64.2 0.0 copy-start.4
  64.3 7.6 %convolution_convert_fusion.1 = bf16[512,3072]{1,0:T(8,128)(2,1)} fusion(bf16[1024,3072]{1,0:T(8,128)(2,1)} %reshape.37, s32[1024]{0:T(1024)S(1)} %bitcast.28), kind=kOutput, calls=%fused_computation.2 | convolution fusion | flops 3223322624 | bytes 9441280 | tf_op jit(solution)/shard_map/dot_general | solution.py:44
  71.8 0.0 reduce-scatter.2.cloned.1.call-update
  71.8 0.0 copy-done.5
  71.9 0.6 dynamic-slice
  73.1 0.0 copy-done.3
  73.1 33.8 %reduce-scatter.2.cloned.1.call-done = bf16[64,3072]{1,0:T(8,128)(2,1)} async-done(((bf16[512,3072]{1,0:T(8,128)(2,1)}), bf16[64,3072]{1,0:T(8,128)(2,1)}) %reduce-scatter.2.cloned.1.call-update) | async-done | bytes 393232 | tf_op jit(solution)/shard_map/reduce_scatter | solution.py:45
  107.0 83.7 %all-reduce.2 = f32[64,3072]{1,0:T(8,128)S(1)} all-reduce(bf16[64,3072]{1,0:T(8,128)(2,1)} %reduce-scatter.2.cloned.1.call-done), channel_id=3, replica_groups=mesh['mode'=8,'member'=16] {'member'}, use_global_device_ids=true, to_apply=%region_1.0.clone | all-reduce | flops 196608 | bytes 1179648
  190.8 0.0 copy-done
  190.8 0.2 fusion.2
  191.0 0.0 copy-done.4
  191.0 0.7 abs_reduce_fusion
  (5 shorter events, 0.1 us)
Async XLA Ops:
  6.5 184.2 %copy-start = (f32[8,6]{1,0:T(8,128)S(1)}, f32[8,6]{1,0:T(8,128)}, u32[]{:S(2)}) copy-start(f32[8,6]{1,0:T(8,128)} %param.14) | copy-start | bytes 580
  6.5 100.4 %reduce-scatter.2.cloned.1.call-start = ((), (), s32[]{:S(2)}) async-start(), calls=%async_computation.1 | async-start | bytes 3538944 | tf_op jit(solution)/shard_map/reduce_scatter | solution.py:45
  52.7 11.5 %copy-start.1 = (s32[1024,1]{0,1:T(1,128)S(1)}, s32[1024,1]{0,1:T(1,128)}, u32[]{:S(2)}) copy-start(s32[1024,1]{0,1:T(1,128)} %param.12) | copy-start | bytes 12292
  52.7 11.5 %copy-start.2 = (s32[1024,1]{0,1:T(1,128)S(1)}, s32[1024,1]{0,1:T(1,128)}, u32[]{:S(2)}) copy-start(s32[1024,1]{0,1:T(1,128)} %param.11) | copy-start | bytes 12292
  64.2 7.6 %copy-start.5 = (u32[128]{0:T(128)S(1)}, u32[128]{0:T(128)}, u32[]{:S(2)}) copy-start(u32[128]{0:T(128)} %constant.11) | copy-start | bytes 1540
  64.2 8.9 %copy-start.3 = (s32[4,8]{1,0:T(4,128)S(1)}, s32[4,8]{1,0:T(4,128)}, u32[]{:S(2)}) copy-start(s32[4,8]{1,0:T(4,128)} %param.13) | copy-start | bytes 388
  64.2 126.7 %copy-start.4 = (f32[4,8]{1,0:T(4,128)S(1)}, f32[4,8]{1,0:T(4,128)}, u32[]{:S(2)}) copy-start(f32[4,8]{1,0:T(4,128)} %param.15) | copy-start | bytes 388
Sparse Core Ops, SparseCore 0:
  72.0 34.9 reduce-scatter.1
where the time goes:
time: 199 us
  blocking collectives  109 us (55%)
  waiting for transfers between devices  33.9 us (17%)
  local copies, waits for them, and re-layouts  24.2 us (12%)
  matrix products  16.2 us (8%)
  between operations  14.2 us (7%)
    unnamed x1, blocking collectives  83.7 us
    reduce_scatter x1, waiting for transfers between devices, local(): lax.psum_scatter(group_part.astype(jnp.bfloat16), 'mode', scatter_dimensi...  33.8 us
    all_gather x1, blocking collectives, local(): modal_resp = lax.all_gather(local_resp, 'member', axis=0, tiled=True)  25.6 us
    reshape x1, local copies, waits for them, and re-layouts, local(): packed = partial.reshape(members_here, comp_count * partial.shape[1])  11.5 us
    convert_element_type x1, local copies, waits for them, and re-layouts, local(): jnp.dot(mode_shapes, modal_resp, preferred_element_type=jnp.float32)  8.68 us
    dot_general x1, matrix products, local(): jnp.dot(mode_shapes, modal_resp, preferred_element_type=jnp.float32)  8.21 us
    dot_general x1, matrix products, local(): group_part = jnp.dot(selector, packed, preferred_element_type=jnp.float32)  7.56 us
  transfers between devices with their start and end apart: 1, of which 1 were waited for; matrix products, arithmetic and copies ran while one was open for 0% of the time, Pallas kernels for 0%

commit v1 on v0

--- a/solution.py
+++ b/solution.py
@@ -2,6 +2,11 @@
 import jax.numpy as jnp
 from jax import lax
 from jax.sharding import PartitionSpec as P
+
+
+def gather_by_exchange(x, axis, dim):
+    copies = jnp.concatenate([x] * lax.axis_size(axis), axis=dim)
+    return lax.all_to_all(copies, axis, dim, dim, tiled=True)
 
 
 def lagged_table(ground_accel, tap_count):
@@ -33,7 +38,7 @@
     local_resp = lax.dot_general(
         modal_kernel[:, ::-1], lagged, (((1,), (1,)), ((), ())), preferred_element_type=jnp.float32
     ).astype(jnp.bfloat16)
-    modal_resp = lax.all_gather(local_resp, "member", axis=0, tiled=True)
+    modal_resp = gather_by_exchange(local_resp, "member", 0)
     partial = jnp.dot(mode_shapes, modal_resp, preferred_element_type=jnp.float32).astype(
         jnp.bfloat16
     )

time: 199 us -> 201 us (1.010)
  blocking collectives: 109 us -> 83.7 us
  waiting for transfers between devices: 33.9 us -> 43.5 us
  local copies, waits for them, and re-layouts: 24.2 us -> 33.4 us
  starting transfers between devices: 0.01 us -> 8.17 us
    all_gather x1 -> x0, blocking collectives: 25.6 us -> none  [local(): modal_resp = lax.all_gather(local_resp, 'member', axis=0, tiled=True)]
    all_to_all x0 -> x1, waiting for transfers between devices: none -> 11.4 us  [gather_by_exchange(): return lax.all_to_all(copies, axis, dim, dim, tiled=True)]
    unnamed x15 -> x29, local copies, waits for them, and re-layouts: 0.71 us -> 9.28 us
    all_to_all x0 -> x1, starting transfers between devices: none -> 8.13 us  [gather_by_exchange(): return lax.all_to_all(copies, axis, dim, dim, tiled=True)]
  transfers between devices with their start and end apart: 1 -> 2, of which waited for: 1 -> 2; matrix products, arithmetic and copies ran while one was open for 0% -> 0% of each run, Pallas kernels for 0% -> 0%
where the time goes in v1:
time: 201 us
  blocking collectives  83.7 us (42%)
  waiting for transfers between devices  43.5 us (22%)
  local copies, waits for them, and re-layouts  33.4 us (17%)
  matrix products  16.9 us (8%)
  between operations  14.2 us (7%)
  starting transfers between devices  8.17 us (4%)
    unnamed x1, blocking collectives  83.7 us
    reduce_scatter x1, waiting for transfers between devices, local(): lax.psum_scatter(group_part.astype(jnp.bfloat16), 'mode', scatter_dimensi...  32 us
    reshape x1, local copies, waits for them, and re-layouts, local(): packed = partial.reshape(members_here, comp_count * partial.shape[1])  11.5 us
    all_to_all x1, waiting for transfers between devices, gather_by_exchange(): return lax.all_to_all(copies, axis, dim, dim, tiled=True)  11.4 us
    unnamed x29, local copies, waits for them, and re-layouts  9.28 us
    convert_element_type x1, local copies, waits for them, and re-layouts, local(): jnp.dot(mode_shapes, modal_resp, preferred_element_type=jnp.float32)  8.68 us
    dot_general x1, matrix products, local(): jnp.dot(mode_shapes, modal_resp, preferred_element_type=jnp.float32)  8.2 us
    all_to_all x1, starting transfers between devices, gather_by_exchange(): return lax.all_to_all(copies, axis, dim, dim, tiled=True)  8.13 us
  transfers between devices with their start and end apart: 2, of which 2 were waited for; matrix products, arithmetic and copies ran while one was open for 0% of the time, Pallas kernels for 0%

profile of v1, /device:TPU:0, one launch (start us, length us, event | category | flops | bytes accessed | tf_op | source)
XLA Modules:
  0.0 200.6 jit_solution(6733868398140942775)
XLA Ops:
  6.5 0.8 tile.4
  7.3 0.6 tile.10
  8.0 0.2 slice.8
  8.2 0.1 copy.21
  8.3 1.6 rev.3
  10.0 0.9 constant_dynamic-update-slice_fusion.15
  10.9 0.6 constant_dynamic-update-slice_fusion.14
  11.5 0.6 constant_dynamic-update-slice_fusion.13
  12.1 0.6 constant_dynamic-update-slice_fusion.12
  12.7 0.6 constant_dynamic-update-slice_fusion.11
  13.3 0.6 constant_dynamic-update-slice_fusion.10
  13.9 0.6 constant_dynamic-update-slice_fusion.9
  14.5 0.6 constant_dynamic-update-slice_fusion.8
  15.2 0.6 constant_dynamic-update-slice_fusion.7
  15.8 0.6 constant_dynamic-update-slice_fusion.6
  16.4 0.6 constant_dynamic-update-slice_fusion.5
  17.0 0.6 constant_dynamic-update-slice_fusion.4
  17.6 0.6 constant_dynamic-update-slice_fusion.3
  18.2 0.6 constant_dynamic-update-slice_fusion.2
  18.8 0.6 constant_dynamic-update-slice_fusion.1
  19.5 0.6 constant_dynamic-update-slice_fusion
  20.1 8.1 %all-to-all-start = ((bf16[16,32,512]{2,1,0:T(8,128)(2,1)}), bf16[16,32,512]{2,1,0:T(8,128)(2,1)S(1)}, u32[]{:S(2)}, u32[]{:S(2)}) async-start(bf16[16,32,512]{2,1,0:T(8,128)(2,1)} %bitcast.2), calls=%async_computation | async-start | bytes 1048576 | tf_op jit(solution)/shard_map/all_to_all | solution.py:9
  28.3 11.4 %all-to-all-done = bf16[16,32,512]{2,1,0:T(8,128)(2,1)S(1)} async-done(((bf16[16,32,512]{2,1,0:T(8,128)(2,1)}), bf16[16,32,512]{2,1,0:T(8,128)(2,1)S(1)}, u32[]{:S(2)}, u32[]{:S(2)}) %all-to-all-start) | async-done | bytes 524320 | tf_op jit(solution)/shard_map/all_to_all | solution.py:9
  39.7 8.2 %fusion = bf16[6144,512]{0,1:T(8,128)(2,1)} fusion(bf16[512,512]{1,0:T(8,128)(2,1)S(1)} %bitcast.30, bf16[6144,512]{1,0:T(8,128)(2,1)} %param.10), kind=kOutput, calls=%fused_computation.1 | convolution fusion | flops 3224371200 | bytes 13107200 | tf_op jit(solution)/shard_map/dot_general | solution.py:42
  47.9 8.7 %copy.14 = bf16[6144,512]{1,0:T(8,128)(2,1)} copy(bf16[6144,512]{0,1:T(8,128)(2,1)} %fusion) | data formatting | bytes 12582912 | tf_op jit(solution)/shard_map/convert_element_type | solution.py:42
  56.6 11.5 %reshape.39 = bf16[1024,3072]{1,0:T(8,128)(2,1)} reshape(bf16[6144,512]{1,0:T(8,128)(2,1)} %copy.14) | data formatting | bytes 12582912 | tf_op jit(solution)/shard_map/reshape | solution.py:46
  68.1 7.6 %convolution_convert_fusion.1 = bf16[512,3072]{1,0:T(8,128)(2,1)} fusion(bf16[1024,3072]{1,0:T(8,128)(2,1)} %reshape.39, s32[1024]{0:T(1024)S(1)} %bitcast.31), kind=kOutput, calls=%fused_computation.2 | convolution fusion | flops 3223322624 | bytes 9441280 | tf_op jit(solution)/shard_map/dot_general | solution.py:49
  75.7 0.6 dynamic-slice
  77.0 32.0 %reduce-scatter.2.cloned.1.call-done = bf16[64,3072]{1,0:T(8,128)(2,1)} async-done(((bf16[512,3072]{1,0:T(8,128)(2,1)}), bf16[64,3072]{1,0:T(8,128)(2,1)}) %reduce-scatter.2.cloned.1.call-update) | async-done | bytes 393232 | tf_op jit(solution)/shard_map/reduce_scatter | solution.py:50
  109.0 83.7 %all-reduce.2 = f32[64,3072]{1,0:T(8,128)S(1)} all-reduce(bf16[64,3072]{1,0:T(8,128)(2,1)} %reduce-scatter.2.cloned.1.call-done), channel_id=3, replica_groups=mesh['mode'=8,'member'=16] {'member'}, use_global_device_ids=true, to_apply=%region_1.0.clone | all-reduce | flops 196608 | bytes 1179648
  192.8 0.2 fusion.2
  193.0 0.7 abs_reduce_fusion
  (19 shorter events, 0.2 us)
Async XLA Ops:
  6.5 186.3 %copy-start = (f32[8,6]{1,0:T(8,128)S(1)}, f32[8,6]{1,0:T(8,128)}, u32[]{:S(2)}) copy-start(f32[8,6]{1,0:T(8,128)} %param.14) | copy-start | bytes 580
  6.5 21.7 %copy-start.2 = (s32[1024,1]{0,1:T(1,128)S(1)}, s32[1024,1]{0,1:T(1,128)}, u32[]{:S(2)}) copy-start(s32[1024,1]{0,1:T(1,128)} %param.11) | copy-start | bytes 12292
  6.5 21.7 %copy-start.1 = (s32[1024,1]{0,1:T(1,128)S(1)}, s32[1024,1]{0,1:T(1,128)}, u32[]{:S(2)}) copy-start(s32[1024,1]{0,1:T(1,128)} %param.12) | copy-start | bytes 12292
  20.1 19.7 %all-to-all-start = ((bf16[16,32,512]{2,1,0:T(8,128)(2,1)}), bf16[16,32,512]{2,1,0:T(8,128)(2,1)S(1)}, u32[]{:S(2)}, u32[]{:S(2)}) async-start(bf16[16,32,512]{2,1,0:T(8,128)(2,1)} %bitcast.2), calls=%async_computation | async-start | bytes 1048576 | tf_op jit(solution)/shard_map/all_to_all | solution.py:9
  28.2 80.8 %reduce-scatter.2.cloned.1.call-start = ((), (), s32[]{:S(2)}) async-start(), calls=%async_computation.2 | async-start | bytes 3538944 | tf_op jit(solution)/shard_map/reduce_scatter | solution.py:50
  68.1 7.6 %copy-start.5 = (u32[128]{0:T(128)S(1)}, u32[128]{0:T(128)}, u32[]{:S(2)}) copy-start(u32[128]{0:T(128)} %constant.11) | copy-start | bytes 1540
  68.1 8.9 %copy-start.3 = (s32[4,8]{1,0:T(4,128)S(1)}, s32[4,8]{1,0:T(4,128)}, u32[]{:S(2)}) copy-start(s32[4,8]{1,0:T(4,128)} %param.13) | copy-start | bytes 388
  68.1 124.9 %copy-start.4 = (f32[4,8]{1,0:T(4,128)S(1)}, f32[4,8]{1,0:T(4,128)}, u32[]{:S(2)}) copy-start(f32[4,8]{1,0:T(4,128)} %param.15) | copy-start | bytes 388
Sparse Core Ops, SparseCore 0:
  75.8 33.1 reduce-scatter.1
